TPU v7x, 256 devices: a whole 4x4x8 slice. The times are simulated.
256 devices in a mesh: req: 64 (over z, x, core), kv: 4 (over y).
Axes of the slice: x: 4, y: 4, z: 8, core: 2. Of those that a mesh axis runs over, the one named last changes fastest.
Arguments:
- residual_in: bfloat16 [128, 2560], P('req', 'kv'), may hold values from -8 to 8
- queries: bfloat16 [128, 2560], P('req', 'kv'), may hold values from -480 to 480
- fresh_token_keys: bfloat16 [128, 512], P('req', 'kv'), may hold values from -6 to 6
- fresh_token_values: bfloat16 [128, 512], P('req', 'kv'), may hold values from -6 to 6
- cached_key_slots: bfloat16 [128, 4096, 512], P('req', None, 'kv'), may hold values from -6 to 6
- cached_value_slots: bfloat16 [128, 4096, 512], P('req', None, 'kv'), may hold values from -6 to 6
- lengths: int32 [128], replicated, may hold values from 1 to 4096, as said below
- slot_order: int32 [128], replicated, may hold values from 0 to 127, as said below
- out_proj: bfloat16 [2560, 2560], P('kv'), may hold values from -0.5 to 0.5
- norm_gain: bfloat16 [2560], P('kv'), may hold values from 0.5 to 1.5
- expert_ids: int32 [128, 6], replicated, may hold values from 0 to 63, all different within a row; in each aligned block of 128 rows (0 to 127, 128 to 255, ...) at most 24 rows name the same one
- gate_values: float32 [128, 6], replicated, may hold values from 0.1 to 0.5
- gate_proj: bfloat16 [64, 2560, 1536], P('req', None, 'kv'), may hold values from -0.125 to 0.125
- up_proj: bfloat16 [64, 2560, 1536], P('req', None, 'kv'), may hold values from -0.125 to 0.125
- down_proj: bfloat16 [64, 1536, 2560], P('req', 'kv'), may hold values from -0.15625 to 0.15625
Outputs:
- layer_out: bfloat16 [128, 2560], P('req', 'kv')
Inputs may be any that keep to these rules, and one draw needn't show every extreme that they name: `lengths`: each request's count of cached positions; some request has exactly 4096. A permutation of the requests: slot s serves request slot_order[s], and cached_key_slots[s], cached_value_slots[s] hold that request's cache. Requests sorted by decreasing length are dealt to the 64 groups of 2 consecutive slots, one round forward, the next backward. `expert_ids`: each token names 6 different experts; no expert is named by more than 24 tokens, a bound that some block reaches.
All inputs are finite; a program needn't handle non-finite values.
Results may differ from a plain program's by a relative error of at most 0.012.
Values may be sent and summed in bfloat16 or wider, within the bound.
No kernel may reach another device: no remote copies, remote signals or barrier semaphores. Data moves between devices by JAX's collectives and lax.ppermute only.
A program may use at most 64 MiB of HBM per device.

v0:
```python
import math
import jax
import jax.numpy as jnp
from jax import lax
from jax.sharding import PartitionSpec as P

COMBINE = "a2a"


def per_device(
    residual_in,
    queries,
    fresh_token_keys,
    fresh_token_values,
    cached_key_slots,
    cached_value_slots,
    lengths,
    slot_order,
    out_proj,
    norm_gain,
    expert_ids,
    gate_values,
    gate_proj,
    up_proj,
    down_proj,
):
    req_count = lax.axis_size("req")
    kv_count = lax.axis_size("kv")
    req_index = lax.axis_index("req")
    kv_index = lax.axis_index("kv")
    per_dev = residual_in.shape[0]
    head_dim = fresh_token_keys.shape[1]
    col_count = residual_in.shape[1]
    total_reqs = lengths.shape[0]
    model_width = out_proj.shape[1]
    q_width = queries.shape[1]
    packed = jnp.concatenate([queries, fresh_token_keys, fresh_token_values, residual_in], axis=1)
    all_packed = lax.all_gather(packed, "req", axis=0, tiled=True)
    served = lax.dynamic_slice_in_dim(slot_order, req_index * per_dev, per_dev)
    mine = all_packed[served]
    query_rows = mine[:, :q_width].reshape(per_dev, -1, head_dim)
    self_key_row = mine[:, q_width : q_width + head_dim]
    self_value_row = mine[:, q_width + head_dim : q_width + 2 * head_dim]
    residual_rows = mine[:, q_width + 2 * head_dim :]
    live_len = lengths[served]
    inv_root = 1.0 / math.sqrt(head_dim)
    scores = (
        jnp.einsum("rqd,rld->rql", query_rows, cached_key_slots, preferred_element_type=jnp.float32)
        * inv_root
    )
    positions = jnp.arange(cached_key_slots.shape[1])
    scores = jnp.where((positions[None, :] < live_len[:, None])[:, None, :], scores, -1e30)
    own_score = (
        jnp.einsum("rqd,rd->rq", query_rows, self_key_row, preferred_element_type=jnp.float32)
        * inv_root
    )
    highest = jnp.maximum(jnp.max(scores, axis=2), own_score)
    weights = jnp.exp(scores - highest[:, :, None])
    own_weight = jnp.exp(own_score - highest)
    totals = jnp.sum(weights, axis=2) + own_weight
    numerator = jnp.einsum(
        "rql,rld->rqd",
        weights.astype(jnp.bfloat16),
        cached_value_slots,
        preferred_element_type=jnp.float32,
    )
    own_low = lax.optimization_barrier(own_weight.astype(jnp.bfloat16)).astype(jnp.float32)
    numerator = numerator + own_low[:, :, None] * self_value_row.astype(jnp.float32)[:, None, :]
    attended = (numerator / totals[:, :, None]).astype(jnp.bfloat16).reshape(per_dev, -1)
    projected = jnp.dot(attended, out_proj, preferred_element_type=jnp.float32)
    col_start = kv_index * col_count
    own_cols = jnp.concatenate(
        [residual_rows.astype(jnp.float32), norm_gain.astype(jnp.float32)[None, :]], axis=0
    )
    summed_in = jnp.concatenate(
        [projected, jnp.zeros((1, model_width), jnp.float32)], axis=0
    ) + lax.dynamic_update_slice(
        jnp.zeros((per_dev + 1, model_width), jnp.float32), own_cols, (0, col_start)
    )
    summed = lax.psum(summed_in, "kv")
    hidden = summed[:per_dev]
    gain = summed[per_dev]
    squares = jnp.sum(hidden * hidden, axis=1)
    normed = (hidden * lax.rsqrt(squares / model_width + 1e-06)[:, None] * gain).astype(
        jnp.bfloat16
    )
    by_slot = lax.all_gather(normed, "req", axis=0, tiled=True)
    slot_of = (
        jnp.zeros((total_reqs,), jnp.int32)
        .at[slot_order]
        .set(jnp.arange(total_reqs, dtype=jnp.int32))
    )
    local_count = gate_proj.shape[0]
    capacity = min(2 * total_reqs * expert_ids.shape[1] // (local_count * req_count), total_reqs)
    expert = req_index * local_count + 0
    named_here = expert_ids == expert
    token_gate = jnp.sum(jnp.where(named_here, gate_values, 0.0), axis=1)
    uses_expert = jnp.any(named_here, axis=1)
    picked = jnp.nonzero(uses_expert, size=capacity, fill_value=0)[0].astype(jnp.int32)
    valid_rows = jnp.arange(capacity) < jnp.sum(uses_expert.astype(jnp.int32))
    row_block = by_slot[slot_of[picked]]
    gate_h = jnp.dot(row_block, gate_proj[0], preferred_element_type=jnp.float32)
    up_h = jnp.dot(row_block, up_proj[0], preferred_element_type=jnp.float32)
    inner_act = (jax.nn.silu(gate_h) * up_h).astype(jnp.bfloat16)
    outputs = jnp.dot(inner_act, down_proj[0], preferred_element_type=jnp.float32)
    row_gate = jnp.where(valid_rows, token_gate[picked], 0.0)
    weighted = outputs * row_gate[:, None]
    weighted = lax.psum_scatter(weighted, "kv", scatter_dimension=1, tiled=True)
    own_hidden = lax.dynamic_slice_in_dim(hidden, col_start, col_count, axis=1)
    combined = (
        jnp.zeros((total_reqs, col_count), jnp.float32)
        .at[picked]
        .add(weighted)
        .at[served]
        .add(own_hidden)
    )
    if COMBINE == "rs":
        layer_rows = lax.psum_scatter(combined, "req", scatter_dimension=0, tiled=True)
    else:
        layer_rows = jnp.sum(
            lax.all_to_all(
                combined.reshape(req_count, per_dev, col_count), "req", 0, 0, tiled=False
            ),
            axis=0,
        )
    return layer_rows.astype(jnp.bfloat16)


def solution(mesh):
    in_specs = (
        P("req", "kv"),
        P("req", "kv"),
        P("req", "kv"),
        P("req", "kv"),
        P("req", None, "kv"),
        P("req", None, "kv"),
        P(),
        P(),
        P("kv", None),
        P("kv"),
        P(),
        P(),
        P("req", None, "kv"),
        P("req", None, "kv"),
        P("req", "kv", None),
    )
    out_specs = P("req", "kv")
    return jax.shard_map(
        per_device, mesh=mesh, in_specs=in_specs, out_specs=out_specs, check_vma=False
    )
```

profile of v0, /device:TPU:1, one launch (start us, length us, event | category | flops | bytes accessed | tf_op | source)
XLA Modules:
  0.0 225.2 jit_solution(8981033612592452208)
XLA Ops:
  6.5 0.0 copy-start
  6.5 0.9 compare_select_fusion.4
  7.4 0.5 copy-done.3
  8.0 0.7 maximum_bitcast_fusion
  8.7 57.9 %all-gather = bf16[64,2,1536]{2,1,0:T(2,128)(2,1)} all-gather(bf16[1,2,1536]{2,1,0:T(2,128)(2,1)S(1)} %maximum_bitcast_fusion), channel_id=1, replica_groups=mesh['req'=64,'kv'=4] {'req'}, dimensions={0}, use_global_device_ids=true | all-gather | bytes 399360 | tf_op jit(solution)/shard_map/all_gather | solution.py:38
  66.6 1.9 reshape.232
  68.5 1.6 gather_fusion.1
  70.2 1.3 gather_fusion
  71.5 0.1 iota_compare_fusion
  71.6 0.1 fusion.40
  71.7 2.3 %fusion.51 = (f32[2,5]{1,0:T(2,128)S(1)}, f32[2,5,4096]{2,1,0:T(8,128)S(1)}) fusion(bf16[2,5,128]{2,1,0:T(8,128)(2,1)S(1)} %reshape.151, bf16[2,4096,128]{2,1,0:T(8,128)(2,1)} %param.19, pred[2,4096]{1,0:T(4,128)(4,1)S(1)} %iota_compare_fusion), kind=kOutput, calls=%fused_computation.85 | convolution fusion | flops 10608630 | bytes 2271784 | tf_op jit(solution)/shard_map/rqd,rld->rql/dot_general | solution.py:48
  74.0 0.2 fusion.17
  74.2 0.6 fusion.48
  74.8 0.6 convert_element_type.49
  75.4 0.7 broadcast_in_dim.69
  76.1 2.0 fusion.16
  78.1 0.0 copy-start.1
  78.1 0.0 copy-start.2
  78.2 0.0 copy-start.4
  78.2 0.5 fusion.37
  78.8 13.9 %psum.7 = f32[3,2560]{1,0:T(4,128)S(1)} all-reduce(f32[3,2560]{1,0:T(4,128)S(1)} %add_dynamic-update-slice_fusion), channel_id=1, replica_groups=mesh['req'=64,'kv'=4] {'kv'}, use_global_device_ids=true, to_apply=%region_7.8 | all-reduce | flops 7680 | bytes 61440 | tf_op jit(solution)/shard_map/psum | solution.py:80
  92.6 0.1 fusion.49
  92.9 0.6 compare_select_fusion.3
  93.5 0.1 fusion.34
  93.6 56.6 %all-gather.1 = bf16[64,2,2560]{2,1,0:T(2,128)(2,1)} all-gather(bf16[1,2,2560]{2,1,0:T(2,128)(2,1)S(1)} %fusion.34), channel_id=1, replica_groups=mesh['req'=64,'kv'=4] {'req'}, dimensions={0}, use_global_device_ids=true | all-gather | bytes 665600 | tf_op jit(solution)/shard_map/all_gather | solution.py:87
  150.2 2.7 %reshape.234 = bf16[128,2560]{1,0:T(8,128)(2,1)} reshape(bf16[64,2,2560]{2,1,0:T(2,128)(2,1)} %all-gather.1) | data formatting | bytes 1310720
  152.9 0.1 copy.36
  153.0 0.2 reduce-window.6
  153.2 0.1 fusion.23
  153.3 1.4 scatter_custom_fusion
  154.7 0.1 copy.37
  154.9 0.8 fusion.32
  155.6 1.0 scatter_custom_fusion.1
  156.6 0.7 gather_fusion.2
  157.3 0.1 copy.38
  157.4 0.1 fusion.33
  157.5 0.7 gather_fusion.4
  158.2 0.7 compare_select_fusion.5
  158.9 1.9 gather_fusion.3
  160.8 1.9 fusion.4
  162.8 3.8 %convolution_multiply_fusion.1 = f32[24,2560]{1,0:T(8,128)} fusion(bf16[1,384,2560]{2,1,0:T(8,128)(2,1)} %param.29, bf16[24,2560]{1,0:T(8,128)(2,1)S(1)} %gather_fusion.3, bf16[1,2560,384]{2,1,0:T(8,128)(2,1)} %param.28, f32[24]{0:T(128)S(1)} %compare_select_fusion.5, f32[24,384]{1,0:T(8,128)S(1)} %fusion.4), kind=kOutput, calls=%fused_computation.11 | convolution fusion | flops 94488576 | bytes 4337760 | tf_op jit(solution)/shard_map/dot_general | solution.py:105
  166.5 0.0 reduce-scatter.2.cloned.1.call-update
  166.5 16.9 %reduce-scatter.2.cloned.1.call-done = f32[24,640]{1,0:T(8,128)} async-done(((f32[24,2560]{1,0:T(8,128)}), f32[24,640]{1,0:T(8,128)}) %reduce-scatter.2.cloned.1.call-update) | async-done | bytes 61456 | tf_op jit(solution)/shard_map/reduce_scatter | solution.py:108
  183.5 1.7 scatter_custom_fusion.2
  185.2 2.4 %scatter_custom_fusion.3 = f32[128,640]{1,0:T(8,128)} fusion(f32[128,640]{1,0:T(8,128)} %scatter_custom_fusion.2, s32[2]{0:T(128)} %copy-done.3, f32[2,2560]{1,0:T(2,128)S(1)} %get-tuple-element.7, s32[]{:T(128)} %constant.31.clone.1, s32[]{:T(128)S(6)} %select_n.104), kind=kCustom, calls=%fused_computation.54 | custom fusion | flops 1280 | bytes 333316 | tf_op jit(solution)/shard_map/scatter-add | solution.py:115
  187.6 1.9 reshape.153
  189.5 27.2 %all_to_all.5 = f32[64,2,640]{2,1,0:T(2,128)} all-to-all(f32[64,2,640]{2,1,0:T(2,128)} %reshape.153), channel_id=1, replica_groups=mesh['req'=64,'kv'=4] {'req'}, dimensions={0} | all-to-all | bytes 655360 | tf_op jit(solution)/shard_map/all_to_all | solution.py:121
  216.7 1.7 reduce_sum.53
  (23 shorter events, 0.2 us)
Async XLA Ops:
  6.5 71.6 %copy-start = (bf16[640,2560]{1,0:T(8,128)(2,1)S(1)}, bf16[640,2560]{1,0:T(8,128)(2,1)}, u32[]{:S(2)}) copy-start(bf16[640,2560]{1,0:T(8,128)(2,1)} %param.23) | copy-start | bytes 9830404
  6.5 176.9 %reduce-scatter.2.cloned.1.call-start = ((), (), s32[]{:S(2)}) async-start(), calls=%async_computation.2 | async-start | bytes 307200 | tf_op jit(solution)/shard_map/reduce_scatter | solution.py:108
  7.4 0.5 copy-start.3
  78.1 14.7 %copy-start.1 = (f32[128,6]{0,1:T(8,128)S(1)}, f32[128,6]{0,1:T(8,128)}, u32[]{:S(2)}) copy-start(f32[128,6]{0,1:T(8,128)} %param.26) | copy-start | bytes 9220
  78.1 14.7 %copy-start.2 = (s32[128,6]{0,1:T(8,128)S(1)}, s32[128,6]{0,1:T(8,128)}, u32[]{:S(2)}) copy-start(s32[128,6]{0,1:T(8,128)} %param.25) | copy-start | bytes 9220
  78.2 14.7 %copy-start.4 = (s32[128]{0:T(128)S(1)}, s32[128]{0:T(128)}, u32[]{:S(2)}) copy-start(s32[128]{0:T(128)} %param.22) | copy-start | bytes 1540
Sparse Core Ops, SparseCore 0:
  166.7 16.7 reduce-scatter.1
where the time goes:
time: 226 us; the launch traced here: 225 us
  blocking collectives  156 us (69%)
  waiting for transfers between devices  17 us (8%)
  local copies, waits for them, and re-layouts  15.3 us (7%)
  between operations  13.6 us (6%)
  other arithmetic  13.1 us (6%)
  matrix products  10.7 us (5%)
    all_gather x1, blocking collectives, per_device(): all_packed = lax.all_gather(packed, 'req', axis=0, tiled=True)  57.9 us
    all_gather x1, blocking collectives, per_device(): by_slot = lax.all_gather(normed, 'req', axis=0, tiled=True)  56.6 us
    all_to_all x1, blocking collectives, per_device(): lax.all_to_all(combined.reshape(req_count, per_dev, col_count), 'req', 0,...  27.2 us
    reduce_scatter x1, waiting for transfers between devices, per_device(): weighted = lax.psum_scatter(weighted, 'kv', scatter_dimension=1, tiled=True)  16.9 us
    psum x1, blocking collectives, per_device(): summed = lax.psum(summed_in, 'kv')  13.9 us
    unnamed x12, local copies, waits for them, and re-layouts  5.18 us
  transfers between devices with their start and end apart: 1, of which 1 were waited for; matrix products, arithmetic and copies ran while one was open for 0% of the time, Pallas kernels for 0%

commit v1 on v0

--- a/solution.py
+++ b/solution.py
@@ -77,7 +77,7 @@
     ) + lax.dynamic_update_slice(
         jnp.zeros((per_dev + 1, model_width), jnp.float32), own_cols, (0, col_start)
     )
-    summed = lax.psum(summed_in, "kv")
+    summed = jnp.sum(lax.all_gather(summed_in, "kv"), axis=0)
     hidden = summed[:per_dev]
     gain = summed[per_dev]
     squares = jnp.sum(hidden * hidden, axis=1)

time: 226 us -> 218 us (0.965)
  blocking collectives: 156 us -> 151 us
    psum x1 -> x0, blocking collectives: 13.9 us -> none  [per_device(): summed = lax.psum(summed_in, 'kv')]
    all_gather x0 -> x1, blocking collectives: none -> 10.2 us  [per_device(): summed = jnp.sum(lax.all_gather(summed_in, 'kv'), axis=0)]
    unnamed x12 -> x14, local copies, waits for them, and re-layouts: 5.18 us -> 4.73 us
where the time goes in v1:
time: 218 us
  blocking collectives  151 us (69%)
  waiting for transfers between devices  18.3 us (8%)
  local copies, waits for them, and re-layouts  14.2 us (7%)
  between operations  13.6 us (6%)
  other arithmetic  12 us (6%)
  matrix products  9.19 us (4%)
    all_gather x1, blocking collectives, per_device(): all_packed = lax.all_gather(packed, 'req', axis=0, tiled=True)  57.9 us
    all_gather x1, blocking collectives, per_device(): by_slot = lax.all_gather(normed, 'req', axis=0, tiled=True)  55.2 us
    all_to_all x1, blocking collectives, per_device(): lax.all_to_all(combined.reshape(req_count, per_dev, col_count), 'req', 0,...  27.2 us
    reduce_scatter x1, waiting for transfers between devices, per_device(): weighted = lax.psum_scatter(weighted, 'kv', scatter_dimension=1, tiled=True)  18.2 us
    all_gather x1, blocking collectives, per_device(): summed = jnp.sum(lax.all_gather(summed_in, 'kv'), axis=0)  10.2 us
    unnamed x14, local copies, waits for them, and re-layouts  4.73 us
  transfers between devices with their start and end apart: 1, of which 1 were waited for; matrix products, arithmetic and copies ran while one was open for 0% of the time, Pallas kernels for 0%

profile of v1, /device:TPU:1, one launch (start us, length us, event | category | flops | bytes accessed | tf_op | source)
XLA Modules:
  0.0 217.7 jit_solution(16429583218855168579)
XLA Ops:
  6.5 0.0 copy-start
  6.5 0.9 compare_select_fusion.4
  7.4 0.8 maximum_bitcast_fusion
  8.3 57.9 %all-gather = bf16[64,2,1536]{2,1,0:T(2,128)(2,1)} all-gather(bf16[1,2,1536]{2,1,0:T(2,128)(2,1)S(1)} %maximum_bitcast_fusion), channel_id=1, replica_groups=mesh['req'=64,'kv'=4] {'req'}, dimensions={0}, use_global_device_ids=true | all-gather | bytes 399360 | tf_op jit(solution)/shard_map/all_gather | solution.py:38
  66.2 1.9 reshape.234
  68.1 1.6 gather_fusion.1
  69.7 1.3 gather_fusion
  71.0 0.1 iota_compare_fusion
  71.1 0.1 fusion.43
  71.2 2.4 %fusion.54 = (f32[2,5]{1,0:T(2,128)S(1)}, f32[2,5,4096]{2,1,0:T(8,128)S(1)}) fusion(bf16[2,5,128]{2,1,0:T(8,128)(2,1)S(1)} %reshape.153, bf16[2,4096,128]{2,1,0:T(8,128)(2,1)} %param.19, pred[2,4096]{1,0:T(4,128)(4,1)S(1)} %iota_compare_fusion), kind=kOutput, calls=%fused_computation.89 | convolution fusion | flops 10608630 | bytes 2271784 | tf_op jit(solution)/shard_map/rqd,rld->rql/dot_general | solution.py:48
  73.7 0.2 fusion.17
  73.9 0.4 fusion.16
  74.4 0.0 copy-done
  74.4 0.0 copy-start.4
  74.4 0.0 copy-start.2
  74.4 0.0 copy-start.3
  74.4 0.0 copy-start.5
  74.4 0.5 fusion.40
  75.0 0.1 copy-done.4
  75.1 10.2 %all_gather.17 = f32[4,3,2560]{2,1,0:T(4,128)S(1)} all-gather(f32[1,3,2560]{2,1,0:T(4,128)S(1)} %fusion.36), channel_id=1, replica_groups=mesh['req'=64,'kv'=4] {'kv'}, dimensions={0}, use_global_device_ids=true | all-gather | bytes 153600 | tf_op jit(solution)/shard_map/all_gather | solution.py:80
  85.3 0.1 fusion.52
  85.5 0.0 copy-done.2
  85.5 0.6 compare_select_fusion.3
  86.2 0.1 fusion.37
  86.3 55.2 %all-gather.1 = bf16[64,2,2560]{2,1,0:T(2,128)(2,1)} all-gather(bf16[1,2,2560]{2,1,0:T(2,128)(2,1)S(1)} %fusion.37), channel_id=1, replica_groups=mesh['req'=64,'kv'=4] {'req'}, dimensions={0}, use_global_device_ids=true | all-gather | bytes 665600 | tf_op jit(solution)/shard_map/all_gather | solution.py:87
  141.5 2.7 %reshape.236 = bf16[128,2560]{1,0:T(8,128)(2,1)} reshape(bf16[64,2,2560]{2,1,0:T(2,128)(2,1)} %all-gather.1) | data formatting | bytes 1310720
  144.2 0.1 copy.36
  144.3 0.2 reduce-window.6
  144.5 0.1 fusion.23
  144.6 1.4 scatter_custom_fusion
  146.0 0.1 copy.37
  146.2 0.8 fusion.32
  147.0 1.0 scatter_custom_fusion.1
  147.9 0.7 gather_fusion.2
  148.6 0.1 copy.38
  148.7 0.1 fusion.33
  148.9 0.7 gather_fusion.4
  149.6 0.7 compare_select_fusion.5
  150.2 1.9 gather_fusion.3
  152.2 1.9 fusion.4
  154.1 3.8 %convolution_multiply_fusion.1 = f32[24,2560]{1,0:T(8,128)} fusion(bf16[1,384,2560]{2,1,0:T(8,128)(2,1)} %param.29, bf16[24,2560]{1,0:T(8,128)(2,1)S(1)} %gather_fusion.3, bf16[1,2560,384]{2,1,0:T(8,128)(2,1)} %param.28, f32[24]{0:T(128)S(1)} %compare_select_fusion.5, f32[24,384]{1,0:T(8,128)S(1)} %fusion.4), kind=kOutput, calls=%fused_computation.11 | convolution fusion | flops 94488576 | bytes 4337760 | tf_op jit(solution)/shard_map/dot_general | solution.py:105
  157.8 0.0 reduce-scatter.2.cloned.1.call-update
  157.9 18.2 %reduce-scatter.2.cloned.1.call-done = f32[24,640]{1,0:T(8,128)} async-done(((f32[24,2560]{1,0:T(8,128)}), f32[24,640]{1,0:T(8,128)}) %reduce-scatter.2.cloned.1.call-update) | async-done | bytes 61456 | tf_op jit(solution)/shard_map/reduce_scatter | solution.py:108
  176.1 1.7 scatter_custom_fusion.2
  177.8 2.2 %scatter_custom_fusion.3 = f32[128,640]{1,0:T(8,128)} fusion(f32[128,640]{1,0:T(8,128)} %scatter_custom_fusion.2, s32[2]{0:T(128)S(1)} %compare_select_fusion.4, f32[2,2560]{1,0:T(2,128)S(1)} %get-tuple-element.7, s32[]{:T(128)} %constant.33.clone.1, s32[]{:T(128)S(6)} %select_n.104), kind=kCustom, calls=%fused_computation.58 | custom fusion | flops 1280 | bytes 333316 | tf_op jit(solution)/shard_map/scatter-add | solution.py:115
  180.1 1.9 reshape.155
  182.0 27.2 %all_to_all.5 = f32[64,2,640]{2,1,0:T(2,128)} all-to-all(f32[64,2,640]{2,1,0:T(2,128)} %reshape.155), channel_id=1, replica_groups=mesh['req'=64,'kv'=4] {'req'}, dimensions={0} | all-to-all | bytes 655360 | tf_op jit(solution)/shard_map/all_to_all | solution.py:121
  209.2 1.7 reduce_sum.63
  (26 shorter events, 0.3 us)
Async XLA Ops:
  6.5 67.8 %copy-start = (bf16[640,2560]{1,0:T(8,128)(2,1)S(1)}, bf16[640,2560]{1,0:T(8,128)(2,1)}, u32[]{:S(2)}) copy-start(bf16[640,2560]{1,0:T(8,128)(2,1)} %param.23) | copy-start | bytes 9830404
  6.5 169.6 %reduce-scatter.2.cloned.1.call-start = ((), (), s32[]{:S(2)}) async-start(), calls=%async_computation.2 | async-start | bytes 307200 | tf_op jit(solution)/shard_map/reduce_scatter | solution.py:108
  71.0 2.9 %copy-start.1 = (bf16[2,4096,128]{2,1,0:T(8,128)(2,1)S(1)}, bf16[2,4096,128]{2,1,0:T(8,128)(2,1)}, u32[]{:S(2)}) copy-start(bf16[2,4096,128]{2,1,0:T(8,128)(2,1)} %param.20) | copy-start | bytes 6291460
  74.4 0.7 copy-start.4
  74.4 11.1 %copy-start.2 = (f32[128,6]{0,1:T(8,128)S(1)}, f32[128,6]{0,1:T(8,128)}, u32[]{:S(2)}) copy-start(f32[128,6]{0,1:T(8,128)} %param.26) | copy-start | bytes 9220
  74.4 11.1 %copy-start.3 = (s32[128,6]{0,1:T(8,128)S(1)}, s32[128,6]{0,1:T(8,128)}, u32[]{:S(2)}) copy-start(s32[128,6]{0,1:T(8,128)} %param.25) | copy-start | bytes 9220
  74.4 11.1 %copy-start.5 = (s32[128]{0:T(128)S(1)}, s32[128]{0:T(128)}, u32[]{:S(2)}) copy-start(s32[128]{0:T(128)} %param.22) | copy-start | bytes 1540
Sparse Core Ops, SparseCore 0:
  158.0 18.0 reduce-scatter.1
